TPU v7x, 512 devices: a whole 4x4x16 slice. The times are simulated.
512 devices in a mesh: row: 32 (over x, z_hi, core), col: 16 (over z_lo, y).
Axes of the slice: x: 4, y: 4, z: 16 (z_hi: 4, z_lo: 4; z = z_hi * 4 + z_lo), core: 2. Of those that a mesh axis runs over, the one named last changes fastest.
Arguments:
- images: bfloat16 [32, 128, 128, 256], P('row', 'col'), may hold values from -6 to 6
- weight: bfloat16 [3, 3, 256, 256], P(None, None, None, 'col'), may hold values from -0.125 to 0.125
- norm_gain: float32 [256], replicated, may hold values from 0.5 to 1.5
- cotangent: bfloat16 [32, 128, 128, 256], P('row', 'col'), may hold values from -6 to 6
Outputs:
- features: bfloat16 [32, 128, 128, 256], P('row', 'col')
- input_grad: bfloat16 [32, 128, 128, 256], P('row', 'col')
- weight_grad: float32 [3, 3, 256, 256], P(None, None, None, 'col')
All inputs are finite; a program needn't handle non-finite values.
Results may differ from a plain program's by a relative error of at most 0.013.
Values may be sent and summed in bfloat16 or wider, within the bound.
No kernel may reach another device: no remote copies, remote signals or barrier semaphores. Data moves between devices by JAX's collectives and lax.ppermute only.
A program may use at most 64 MiB of HBM per device.

v0:
```python
import math
import jax
import jax.numpy as jnp
from jax import lax
from jax.sharding import PartitionSpec as P

epsilon = 1e-06
root_half = 0.7071067811865476
norm_const = 0.3989422804014327


def padded_2(value, sides, width):
    for axis, dim in sides:
        peers, length = (lax.axis_size(axis), value.shape[dim])
        up = [(i, (i + 1) % peers) for i in range(peers - 1)]
        down = [(j, i) for i, j in up]
        last = lax.slice_in_dim(value, length - width, length, axis=dim)
        initial = lax.slice_in_dim(value, 0, width, axis=dim)
        before = lax.ppermute(last, axis, up)
        after = lax.ppermute(initial, axis, down)
        value = jnp.concatenate([before, value, after], axis=dim)
    return value


def norm_act(conv_out, upper, norm_gain):
    mean_val = jnp.mean(conv_out, axis=-1, keepdims=True)
    centred = conv_out - mean_val
    variance = jnp.mean(centred * centred, axis=-1, keepdims=True)
    inv_std = lax.rsqrt(variance + epsilon)
    unit = centred * inv_std
    normed = unit * norm_gain
    cdf_val = 0.5 * (1.0 + lax.erf(normed * root_half))
    density = jnp.exp(-0.5 * normed * normed) * norm_const
    outputs = (normed * cdf_val).astype(jnp.bfloat16)
    upstream = upper.astype(jnp.float32) * (cdf_val + normed * density) * norm_gain
    mean_up = jnp.mean(upstream, axis=-1, keepdims=True)
    mean_cross = jnp.mean(upstream * unit, axis=-1, keepdims=True)
    grad_pre = inv_std * (upstream - mean_up - unit * mean_cross)
    return (outputs, grad_pre.astype(jnp.bfloat16))


def window(padded, tap_row, tap_col, tile_rows, tile_cols):
    return padded[:, tap_row : tap_row + tile_rows, tap_col : tap_col + tile_cols, :].reshape(
        -1, padded.shape[-1]
    )


def on_device(images, weight, norm_gain, cotangent):
    img_count, tile_rows, tile_cols, in_chan = images.shape
    whole_kernel = lax.all_gather(weight, "col", axis=3, tiled=True)
    out_chan = whole_kernel.shape[3]
    rimmed = padded_2(images, (("col", 1),), 1)
    padded = jnp.pad(rimmed, ((0, 0), (0, 0), (1, 1), (0, 0)))
    conv_out = jnp.zeros((img_count * tile_rows * tile_cols, out_chan), jnp.float32)
    for tap_row in range(3):
        for tap_col in range(3):
            conv_out = conv_out + jnp.dot(
                window(padded, tap_row, tap_col, tile_rows, tile_cols),
                whole_kernel[tap_row, tap_col],
                preferred_element_type=jnp.float32,
            )
    outputs, grad_pre = norm_act(conv_out, cotangent.reshape(-1, out_chan), norm_gain)
    grad_grid = grad_pre.reshape(img_count, tile_rows, tile_cols, out_chan)
    grad_rimmed = padded_2(grad_grid, (("col", 1),), 1)
    grad_pad = jnp.pad(grad_rimmed, ((0, 0), (0, 0), (1, 1), (0, 0)))
    grad_input = jnp.zeros((img_count * tile_rows * tile_cols, in_chan), jnp.float32)
    pieces = []
    for tap_row in range(3):
        for tap_col in range(3):
            grad_input = grad_input + lax.dot_general(
                window(grad_pad, 2 - tap_row, 2 - tap_col, tile_rows, tile_cols),
                whole_kernel[tap_row, tap_col],
                (((1,), (1,)), ((), ())),
                preferred_element_type=jnp.float32,
            )
            pieces.append(
                lax.dot_general(
                    window(padded, tap_row, tap_col, tile_rows, tile_cols),
                    grad_pre,
                    (((0,), (0,)), ((), ())),
                    preferred_element_type=jnp.float32,
                )
            )
    partial_value = jnp.stack(pieces).reshape(3, 3, in_chan, out_chan)
    totals = lax.psum(partial_value, ("row", "col"))
    col_share = out_chan // lax.axis_size("col")
    own_share = lax.dynamic_slice_in_dim(totals, lax.axis_index("col") * col_share, col_share, 3)
    pixels = img_count * lax.axis_size("row") * tile_rows * lax.axis_size("col") * tile_cols
    weight_grad = own_share * (1.0 / math.sqrt(pixels))
    features = outputs.reshape(img_count, tile_rows, tile_cols, out_chan)
    input_grad = grad_input.astype(jnp.bfloat16).reshape(img_count, tile_rows, tile_cols, in_chan)
    return (features, input_grad, weight_grad)


def solution(mesh):
    placed = (
        P("row", "col", None, None),
        P(None, None, None, "col"),
        P(),
        P("row", "col", None, None),
    )
    return jax.shard_map(
        on_device,
        mesh=mesh,
        in_specs=placed,
        out_specs=(
            P("row", "col", None, None),
            P("row", "col", None, None),
            P(None, None, None, "col"),
        ),
        check_vma=False,
    )
```

profile of v0, /device:TPU:2, one launch (start us, length us, event | category | flops | bytes accessed | tf_op | source)
XLA Modules:
  0.0 616.7 jit_solution(12036107945683514388)
XLA Ops:
  7.2 0.0 copy-start
  7.2 0.0 all-gather.2.cloned.1.call-start
  7.2 0.7 all-gather.2.cloned.1.call-update
  7.9 0.0 all-reduce.4.cloned.1.call-start
  8.0 0.9 fusion.29
  8.8 3.5 collective-permute-start
  12.3 1.3 collective-permute-start.1
  13.6 0.6 collective-permute-done
  14.2 4.3 collective-permute-done.1
  18.5 1.2 select_maximum_fusion.2
  19.7 0.0 copy-done
  19.7 1.0 pad_maximum_fusion.2
  20.8 1.4 fusion.27
  22.1 79.2 %all-gather.2.cloned.1.call-done = bf16[3,3,256,256]{2,3,1,0:T(8,128)(2,1)} async-done(((bf16[3,3,256,16]{2,3,1,0:T(8,128)(2,1)}), bf16[3,3,256,256]{2,3,1,0:T(8,128)(2,1)}) %all-gather.2.cloned.1.call-update) | async-done | bytes 1179664 | tf_op jit(solution)/shard_map/all_gather | solution.py:50
  101.3 1.4 fusion.21
  102.7 0.0 copy-done.1
  102.7 0.3 fusion.23
  103.0 0.3 convolution_add_fusion.13
  103.4 0.0 copy-start.5
  103.4 0.7 copy-done.6
  104.0 0.3 convolution_add_fusion.12
  104.4 0.1 copy-done.5
  104.4 0.3 convolution_add_fusion.11
  104.8 0.0 copy-start.4
  104.8 0.3 convolution_add_fusion.10
  105.1 0.7 copy-done.4
  105.8 0.3 convolution_add_fusion.9
  106.2 0.3 convolution_add_fusion.8
  106.5 0.7 copy-done.7
  107.2 0.4 fusion.30
  107.6 0.0 copy-start.9
  107.7 0.4 multiply_reduce_fusion.1
  108.1 0.6 copy-done.9
  108.7 1.9 fusion.24
  110.6 0.8 multiply_convert_fusion
  111.5 1.0 fusion.12
  112.5 1.1 fusion.11
  113.5 1.1 fusion.10
  114.6 1.1 fusion.9
  115.7 1.0 fusion.8
  116.7 1.0 fusion.7
  117.8 1.0 fusion.6
  118.8 1.0 fusion.5
  119.8 3.0 collective-permute-start.2
  122.9 1.3 collective-permute-start.3
  124.2 1.0 fusion.4
  125.2 3.1 copy.8
  128.4 0.0 all-reduce.4.cloned.1.call-update
  128.4 0.0 collective-permute-done.2
  128.4 0.6 collective-permute-done.3
  129.0 0.2 select_maximum_fusion
  129.2 0.4 fusion.26
  129.6 0.1 pad_maximum_fusion
  129.7 0.3 fusion.20
  130.0 0.3 fusion.22
  130.3 0.3 convolution_add_fusion.6
  130.6 0.3 convolution_add_fusion.5
  130.9 0.3 convolution_add_fusion.4
  131.2 0.3 convolution_add_fusion.3
  131.5 0.3 convolution_add_fusion.2
  131.8 0.3 convolution_add_fusion.1
  132.1 1.1 fusion.3
  133.2 475.1 %all-reduce.4.cloned.1.call-done = f32[3,3,256,256]{2,3,1,0:T(8,128)} async-done(((f32[3,3,256,256]{2,3,1,0:T(8,128)}), f32[3,3,256,256]{2,3,1,0:T(8,128)}) %all-reduce.4.cloned.1.call-update) | async-done | bytes 2359312 | tf_op jit(solution)/shard_map/psum | solution.py:85
  608.3 1.6 dynamic-slice_multiply_fusion
  (15 shorter events, 0.0 us)
Async XLA Ops:
  7.2 12.6 %copy-start = (bf16[1,8,128,256]{3,2,1,0:T(8,128)(2,1)S(1)}, bf16[1,8,128,256]{3,2,1,0:T(8,128)(2,1)}, u32[]{:S(2)}) copy-start(bf16[1,8,128,256]{3,2,1,0:T(8,128)(2,1)} %param.4) | copy-start | bytes 1572868
  7.2 94.1 %all-gather.2.cloned.1.call-start = ((), (), s32[]{:S(2)}) async-start(), calls=%async_computation | async-start | bytes 1253376 | tf_op jit(solution)/shard_map/all_gather | solution.py:50
  7.9 600.3 %all-reduce.4.cloned.1.call-start = ((), (), s32[]{:S(2)}) async-start(), calls=%async_computation.1 | async-start | bytes 4718592 | tf_op jit(solution)/shard_map/psum | solution.py:85
  8.8 5.4 collective-permute-start
  12.3 6.2 collective-permute-start.1
  22.1 84.1 %copy-start.2 = (bf16[1,8,128,256]{3,2,1,0:T(8,128)(2,1)}, bf16[1,8,128,256]{3,2,1,0:T(8,128)(2,1)S(1)}, u32[]{:S(2)}) copy-start(bf16[1,8,128,256]{3,2,1,0:T(8,128)(2,1)S(1)} %get-tuple-element.13) | copy-start | bytes 1572868
  101.3 1.4 copy-start.1
  101.3 1.7 copy-start.8
  103.0 1.0 copy-start.6
  103.4 1.1 copy-start.5
  104.8 1.0 copy-start.4
  106.2 1.0 copy-start.7
  107.2 0.8 copy-start.10
  107.6 1.0 copy-start.9
  115.7 2.1 copy-start.3
  119.8 8.6 %collective-permute-start.2 = (bf16[1,1,128,256]{3,2,1,0:T(8,128)(2,1)S(1)}, bf16[1,1,128,256]{3,2,1,0:T(8,128)(2,1)S(1)}, u32[]{:S(2)}, u32[]{:S(2)}) collective-permute-start(bf16[1,1,128,256]{3,2,1,0:T(8,128)(2,1)S(1)} %get-tuple-element.21), channel_id=1, source_target_pairs={{0,1},{1,2},{2,3},{3,4},{4,5},{5,6},{6,7},{7,8},{8,9},{9,10},{10,1... | collective-permute-start | bytes 196616 | tf_op jit(solution)/shard_map/ppermute | solution.py:19
  122.9 6.2 collective-permute-start.3
Sparse Core Ops, SparseCore 0:
  10.1 91.1 all-gather.1
  128.5 479.7 all-reduce.3
where the time goes:
time: 617 us
  waiting for transfers between devices  560 us (91%)
  matrix products  17 us (3%)
  between operations  14.3 us (2%)
  starting transfers between devices  9.17 us (1%)
  local copies, waits for them, and re-layouts  8.58 us (1%)
  other arithmetic  7.21 us (1%)
    psum x1, waiting for transfers between devices, on_device(): totals = lax.psum(partial_value, ('row', 'col'))  475 us
    all_gather x1, waiting for transfers between devices, on_device(): whole_kernel = lax.all_gather(weight, 'col', axis=3, tiled=True)  79.2 us
  transfers between devices with their start and end apart: 6, of which 5 were waited for; matrix products, arithmetic and copies ran while one was open for 2% of the time, Pallas kernels for 0%

commit v1 on v0

--- a/solution.py
+++ b/solution.py
@@ -7,6 +7,11 @@
 epsilon = 1e-06
 root_half = 0.7071067811865476
 norm_const = 0.3989422804014327
+
+
+def by_each_axis(value_2, axis_one, axis_two):
+    half = lax.psum(value_2, axis_one)
+    return lax.psum(half, axis_two)
 
 
 def padded_2(value, sides, width):
@@ -82,7 +87,7 @@
                 )
             )
     partial_value = jnp.stack(pieces).reshape(3, 3, in_chan, out_chan)
-    totals = lax.psum(partial_value, ("row", "col"))
+    totals = by_each_axis(partial_value, "row", "col")
     col_share = out_chan // lax.axis_size("col")
     own_share = lax.dynamic_slice_in_dim(totals, lax.axis_index("col") * col_share, col_share, 3)
     pixels = img_count * lax.axis_size("row") * tile_rows * lax.axis_size("col") * tile_cols

time: 617 us -> 664 us (1.076)
  waiting for transfers between devices: 560 us -> 605 us
    psum x1 -> x2, waiting for transfers between devices: 475 us -> 515 us  [the longest x1 330 us: by_each_axis(): half = lax.psum(value_2, axis_one)]
  transfers between devices with their start and end apart: 6 -> 7, of which waited for: 5 -> 7; matrix products, arithmetic and copies ran while one was open for 2% -> 1% of each run, Pallas kernels for 0% -> 0%
where the time goes in v1:
time: 664 us
  waiting for transfers between devices  605 us (91%)
  matrix products  16.9 us (3%)
  between operations  14.1 us (2%)
  local copies, waits for them, and re-layouts  11.2 us (2%)
  starting transfers between devices  9.21 us (1%)
  other arithmetic  7.23 us (1%)
    psum x1, waiting for transfers between devices, by_each_axis(): half = lax.psum(value_2, axis_one)  330 us
    psum x1, waiting for transfers between devices, by_each_axis(): return lax.psum(half, axis_two)  186 us
    all_gather x1, waiting for transfers between devices, on_device(): whole_kernel = lax.all_gather(weight, 'col', axis=3, tiled=True)  79.2 us
  transfers between devices with their start and end apart: 7, of which 7 were waited for; matrix products, arithmetic and copies ran while one was open for 1% of the time, Pallas kernels for 0%

profile of v1, /device:TPU:2, one launch (start us, length us, event | category | flops | bytes accessed | tf_op | source)
XLA Modules:
  0.0 663.7 jit_solution(10248189167685522920)
XLA Ops:
  7.2 0.0 all-gather.2.cloned.1.call-start
  7.2 0.7 all-gather.2.cloned.1.call-update
  7.9 0.0 all-reduce.5.cloned.1.call-start
  8.0 0.9 fusion.29
  8.8 3.5 collective-permute-start
  12.3 1.3 collective-permute-start.1
  13.6 0.6 collective-permute-done
  14.2 4.3 collective-permute-done.1
  18.5 1.2 select_maximum_fusion.2
  19.7 1.0 pad_maximum_fusion.2
  20.8 1.4 fusion.27
  22.1 79.2 %all-gather.2.cloned.1.call-done = bf16[3,3,256,256]{2,3,1,0:T(8,128)(2,1)} async-done(((bf16[3,3,256,16]{2,3,1,0:T(8,128)(2,1)}), bf16[3,3,256,256]{2,3,1,0:T(8,128)(2,1)}) %all-gather.2.cloned.1.call-update) | async-done | bytes 1179664 | tf_op jit(solution)/shard_map/all_gather | solution.py:55
  101.3 1.4 fusion.21
  102.7 0.3 fusion.23
  103.0 0.3 convolution_add_fusion.13
  103.4 0.7 copy-done.6
  104.0 0.3 convolution_add_fusion.12
  104.4 0.1 copy-done.5
  104.4 0.3 convolution_add_fusion.11
  104.8 0.3 convolution_add_fusion.10
  105.1 0.7 copy-done.4
  105.8 0.3 convolution_add_fusion.9
  106.2 0.3 convolution_add_fusion.8
  106.5 0.7 copy-done.11
  107.2 0.4 fusion.30
  107.7 0.4 multiply_reduce_fusion.1
  108.1 0.6 copy-done.13
  108.7 1.9 fusion.24
  110.6 0.8 multiply_convert_fusion
  111.5 1.0 fusion.12
  112.5 1.0 fusion.11
  113.5 1.0 fusion.10
  114.5 1.0 fusion.9
  115.6 1.1 fusion.8
  116.7 1.0 fusion.7
  117.7 1.0 fusion.6
  118.7 1.1 fusion.5
  119.8 1.0 fusion.4
  120.8 3.0 copy.8
  123.9 0.0 all-reduce.5.cloned.1.call-update
  123.9 0.0 all-reduce.7.cloned.1.call-start
  124.0 3.0 collective-permute-start.2
  127.0 1.3 collective-permute-start.3
  128.3 0.6 collective-permute-done.2
  128.9 4.3 collective-permute-done.3
  133.2 0.2 select_maximum_fusion
  133.3 1.6 fusion.26
  134.9 0.3 fusion.20
  135.2 329.7 %all-reduce.5.cloned.1.call-done = f32[3,3,256,256]{2,3,1,0:T(8,128)} async-done(((f32[3,3,256,256]{2,3,1,0:T(8,128)}), f32[3,3,256,256]{2,3,1,0:T(8,128)}) %all-reduce.5.cloned.1.call-update) | async-done | bytes 2359312 | tf_op jit(solution)/shard_map/psum | solution.py:13
  464.9 0.1 pad_maximum_fusion
  465.0 0.3 fusion.22
  465.3 0.3 convolution_add_fusion.6
  465.6 0.7 copy-done.10
  466.3 0.3 convolution_add_fusion.5
  466.6 0.0 copy-done.9
  466.7 0.3 convolution_add_fusion.4
  467.0 0.3 convolution_add_fusion.3
  467.3 0.7 copy-done.8
  468.0 0.3 convolution_add_fusion.2
  468.3 0.1 copy-done.7
  468.4 0.3 convolution_add_fusion.1
  468.7 1.1 fusion.3
  469.8 185.8 %all-reduce.7.cloned.1.call-done = f32[3,3,256,256]{2,3,1,0:T(8,128)} async-done(((f32[3,3,256,256]{2,3,1,0:T(8,128)}), f32[3,3,256,256]{2,3,1,0:T(8,128)}) %all-reduce.7.cloned.1.call-update) | async-done | bytes 2359312 | tf_op jit(solution)/shard_map/psum | solution.py:14
  655.6 1.6 dynamic-slice_multiply_fusion
  (26 shorter events, 0.1 us)
Async XLA Ops:
  7.2 12.6 %copy-start = (bf16[1,8,128,256]{3,2,1,0:T(8,128)(2,1)S(1)}, bf16[1,8,128,256]{3,2,1,0:T(8,128)(2,1)}, u32[]{:S(2)}) copy-start(bf16[1,8,128,256]{3,2,1,0:T(8,128)(2,1)} %param.4) | copy-start | bytes 1572868
  7.2 94.1 %all-gather.2.cloned.1.call-start = ((), (), s32[]{:S(2)}) async-start(), calls=%async_computation | async-start | bytes 1253376 | tf_op jit(solution)/shard_map/all_gather | solution.py:55
  7.9 457.0 %all-reduce.5.cloned.1.call-start = ((), (), s32[]{:S(2)}) async-start(), calls=%async_computation.1 | async-start | bytes 4718592 | tf_op jit(solution)/shard_map/psum | solution.py:13
  8.8 5.4 collective-permute-start
  12.3 6.2 collective-permute-start.1
  22.1 84.0 %copy-start.2 = (bf16[1,8,128,256]{3,2,1,0:T(8,128)(2,1)}, bf16[1,8,128,256]{3,2,1,0:T(8,128)(2,1)S(1)}, u32[]{:S(2)}) copy-start(bf16[1,8,128,256]{3,2,1,0:T(8,128)(2,1)S(1)} %get-tuple-element.13) | copy-start | bytes 1572868
  101.3 1.4 copy-start.1
  101.3 1.7 copy-start.12
  103.0 1.0 copy-start.6
  103.4 1.1 copy-start.5
  104.8 1.0 copy-start.4
  106.2 1.0 copy-start.11
  107.2 0.8 copy-start.14
  107.6 1.0 copy-start.13
  115.6 2.1 copy-start.3
  123.9 531.7 %all-reduce.7.cloned.1.call-start = ((), (), s32[]{:S(2)}) async-start(), calls=%async_computation.2 | async-start | bytes 4718592 | tf_op jit(solution)/shard_map/psum | solution.py:14
  124.0 4.9 collective-permute-start.2
  127.0 6.2 collective-permute-start.3
  465.3 1.0 copy-start.10
  465.6 1.1 copy-start.9
  467.0 1.0 copy-start.8
  467.3 1.1 copy-start.7
Sparse Core Ops, SparseCore 0:
  10.1 91.1 all-gather.1
  124.0 340.8 all-reduce.4
  467.8 187.6 all-reduce.6
